TPU v7x, 32 devices: a whole 2x2x4 slice. The times are simulated.
32 devices in a mesh: test: 4 (over z), cell: 8 (over y, x, core).
Axes of the slice: x: 2, y: 2, z: 4, core: 2. Of those that a mesh axis runs over, the one named last changes fastest.
Arguments:
- log_perm: float32 [128, 16, 256], P('cell'), may hold values from -1 to 1
- panel: float32 [8, 128, 16, 256], P('test', 'cell'), may hold values from -4 to 4
- wells: int32 [4, 8], P('test'), may hold values from 0 to 524287
- rates: float32 [4, 8], P('test'), may hold values from 1 to 10
- recharge: float32 [4, 128, 16, 256], P('test', 'cell'), may hold values from 0.25 to 4
- gauge: float32 [128, 16, 256], P('cell'), may hold values from 0.25 to 4
Outputs:
- hessian_panel: float32 [8, 128, 16, 256], P('test', 'cell')
Inputs may be any that keep to these rules, and one draw needn't show every extreme that they name: `wells`: each entry names a cell of the whole grid, numbered x * 16 * 256 + y * 256 + z; a test may name a cell more than once.
All inputs are finite; a program needn't handle non-finite values.
Results may differ from a plain program's by a relative error of at most 0.0001.
Values sent between devices are 32-bit elements; how exact they have to be, the bound alone decides.
No kernel may reach another device: no remote copies, remote signals or barrier semaphores. Data moves between devices by JAX's collectives and lax.ppermute only.
A program may use at most 64 MiB of HBM per device.

v0:
```python
import math
import jax
import jax.numpy as jnp
import numpy as np
from jax import lax
from jax.sharding import PartitionSpec as P

CHEB = 4
storage = 0.02


def with_halo(cells, sides, width):
    for axis, dim in sides:
        count = lax.axis_size(axis)
        ends = count - 1
        head = lax.slice_in_dim(cells, 0, width, axis=dim)
        tail = lax.slice_in_dim(cells, cells.shape[dim] - width, cells.shape[dim], axis=dim)
        cells = jnp.concatenate(
            [
                lax.ppermute(tail, axis, [(i, (i + 1) % count) for i in range(ends)]),
                cells,
                lax.ppermute(head, axis, [((i + 1) % count, i) for i in range(ends)]),
            ],
            axis=dim,
        )
    return cells


def cheb_table(count):
    highest = storage + 12.0 * math.e
    theta = 0.5 * (highest + storage)
    spread = 0.5 * (highest - storage)
    sigma = theta / spread
    rho = 1.0 / sigma
    keeps = []
    pushes = []
    for turn in range(count):
        after = 1.0 / (2.0 * sigma - rho)
        keeps.append(after * rho)
        pushes.append(2.0 * after / spread)
        rho = after
    return (1.0 / theta, keeps, pushes)


def neighbours(field, back):
    axis = field.ndim - back
    widths = [(0, 0)] * field.ndim
    widths[axis] = (1, 1)
    padded = jnp.pad(field, widths)
    length = field.shape[axis]
    return (
        lax.slice_in_dim(padded, 2, length + 2, axis=axis),
        lax.slice_in_dim(padded, 0, length, axis=axis),
    )


def diffuse(weight_ext, field_ext):
    weight = weight_ext[..., 1:-1, :, :]
    field = field_ext[..., 1:-1, :, :]
    total = 0.5 * (weight + weight_ext[..., 2:, :, :]) * (field - field_ext[..., 2:, :, :])
    total = total + 0.5 * (weight + weight_ext[..., :-2, :, :]) * (
        field - field_ext[..., :-2, :, :]
    )
    for back in (2, 1):
        weight_up, weight_down = neighbours(weight, back)
        field_up, field_down = neighbours(field, back)
        total = (
            total
            + 0.5 * (weight + weight_up) * (field - field_up)
            + 0.5 * (weight + weight_down) * (field - field_down)
        )
    return total


def pairs(left_ext, right_ext):
    left = left_ext[..., 1:-1, :, :]
    right = right_ext[..., 1:-1, :, :]
    total = (left - left_ext[..., 2:, :, :]) * (right - right_ext[..., 2:, :, :])
    total = total + (left - left_ext[..., :-2, :, :]) * (right - right_ext[..., :-2, :, :])
    for back in (2, 1):
        left_up, left_down = neighbours(left, back)
        right_up, right_down = neighbours(right, back)
        total = (
            total
            + (left - left_up) * (right - right_up)
            + (left - left_down) * (right - right_down)
        )
    return total


def rims(field):
    return with_halo(field, (("cell", 1),), 1)


def shards(log_perm, panel, wells, rates, recharge, gauge):
    place = lax.axis_index("cell")
    slab, rows_y, depth_z = log_perm.shape
    tests_here, well_count = wells.shape
    first, keeps, pushes = cheb_table(CHEB)
    keep_table = jnp.asarray(np.array(keeps, np.float32))
    push_table = jnp.asarray(np.array(pushes, np.float32))
    columns = lax.all_gather(panel, "test", axis=0, tiled=True)
    columns_all = columns.shape[0]
    perm = jnp.exp(log_perm)
    stacked = jnp.concatenate([perm[None], perm[None] * columns], axis=0)
    coeff_ext = with_halo(stacked, (("cell", 1),), 2)
    perm_ext = coeff_ext[0]
    scaled_ext = coeff_ext[1:, 1:-1]
    cells = slab * rows_y * depth_z
    flat = place * cells + jnp.arange(cells, dtype=jnp.int32)
    hits = wells[:, :, None] == flat[None, None, :]
    points = jnp.sum(jnp.where(hits, rates[:, :, None], 0.0), axis=1).reshape(
        tests_here, slab, rows_y, depth_z
    )
    counts = jnp.sum(hits.astype(jnp.float32), axis=1).reshape(tests_here, slab, rows_y, depth_z)
    source = recharge + points
    observe = gauge[None] + counts

    def solve(right_side):
        solution = jnp.zeros_like(right_side)
        residual = right_side
        direction = right_side * first

        def sweep(turn, carry):
            solution, residual, direction = carry
            extended = with_halo(direction, (("cell", 1),), 1)
            image = storage * direction + diffuse(perm_ext[1:-1], extended)
            solution = solution + direction
            residual = residual - image
            direction = keep_table[turn] * direction + push_table[turn] * residual
            return (solution, residual, direction)

        solution, residual, direction = lax.fori_loop(
            0, CHEB, sweep, (solution, residual, direction)
        )
        return solution + direction

    state = solve(source)
    state_ext = rims(state)
    forcing = -diffuse(scaled_ext, state_ext[:, None])
    forcing = forcing.reshape(tests_here * columns_all, slab, rows_y, depth_z)
    change = solve(forcing)
    weighted = (
        change.reshape(tests_here, columns_all, slab, rows_y, depth_z) * observe[:, None]
    ).reshape(tests_here * columns_all, slab, rows_y, depth_z)
    adjoint = solve(weighted)
    adjoint_ext = rims(adjoint).reshape(tests_here, columns_all, slab + 2, rows_y, depth_z)
    contrib = jnp.sum(pairs(state_ext[:, None], adjoint_ext), axis=0)
    partial_value = -0.5 * perm[None] * contrib
    total = lax.psum(partial_value, "test")
    share = panel.shape[0]
    owned = lax.dynamic_slice_in_dim(total, lax.axis_index("test") * share, share, 0)
    return owned


def solution(mesh):
    return jax.shard_map(
        shards,
        mesh=mesh,
        in_specs=(
            P("cell", None, None),
            P("test", "cell", None, None),
            P("test", None),
            P("test", None),
            P("test", "cell", None, None),
            P("cell", None, None),
        ),
        out_specs=P("test", "cell", None, None),
        check_vma=False,
    )
```

profile of v0, /device:TPU:0, one launch (start us, length us, event | category | flops | bytes accessed | tf_op | source)
XLA Modules:
  0.0 408.5 jit_solution(683576134354521020)
XLA Ops:
  7.3 1.7 broadcast_multiply_fusion.14
  9.1 48.2 %all-gather.2.cloned.1.call-done = f32[8,16,16,256]{3,2,1,0:T(8,128)} async-done(((f32[2,16,16,256]{3,2,1,0:T(8,128)}), f32[8,16,16,256]{3,2,1,0:T(8,128)}) %all-gather.2.cloned.1.call-update) | async-done | bytes 2097168 | tf_op jit(solution)/shard_map/all_gather | solution.py:102
  57.3 2.0 broadcast_multiply_fusion.6
  60.2 1.3 collective-permute-start.6
  61.4 3.0 collective-permute-start.7
  64.5 1.7 fusion.86
  66.3 1.8 broadcast_multiply_fusion.13
  70.8 51.1 %while.63 = (s32[]{:T(128)}, f32[1,16,16,256]{3,2,1,0:T(8,128)}, f32[1,16,16,256]{3,2,1,0:T(8,128)}, f32[1,16,16,256]{3,2,1,0:T(8,128)}, f32[16,16,256]{2,1,0:T(...) while((s32[]{:T(128)}, f32[1,16,16,256]{3,2,1,0:T(8,128)}, ...), condition=%wide.region_2.3_spmd.clone.clone, body=%wide.region_1.2_spmd.sunk.clone.clone.sunk | while | flops 2424835 | bytes 3637479 | solution.py:133
  71.7 3.3 collective-permute-start
  75.0 1.3 collective-permute-start.1
  77.6 2.4 collective-permute-done.1
  80.0 3.5 multiply_add_fusion.6
  84.4 4.4 %collective-permute-start = (f32[1,1,16,256]{3,2,1,0:T(8,128)S(1)}, f32[1,1,16,256]{3,2,1,0:T(8,128)S(1)}, u32[]{:S(2)}, u32[]{:S(2)}) collective-permute-start(f32[1,1,16,256]{3,2,1,0:T(8,128)S(1)} %get-tuple-element.979), channel_id=1, source_target_pairs={{0,1},{1,2},{2,3},{3,4},{4,5},{5,6},{6,7},{8,9},{9,10},{10,11},{11... | collective-permute-start | bytes 49160 | tf_op jit(solution)/shard_map/while/body/eval_jaxpr/ppermute | solution.py:20
  88.8 1.3 collective-permute-start.1
  92.1 3.6 multiply_add_fusion.6
  96.7 6.0 %collective-permute-start = (f32[1,1,16,256]{3,2,1,0:T(8,128)S(1)}, f32[1,1,16,256]{3,2,1,0:T(8,128)S(1)}, u32[]{:S(2)}, u32[]{:S(2)}) collective-permute-start(f32[1,1,16,256]{3,2,1,0:T(8,128)S(1)} %get-tuple-element.979), channel_id=1, source_target_pairs={{0,1},{1,2},{2,3},{3,4},{4,5},{5,6},{6,7},{8,9},{9,10},{10,11},{11... | collective-permute-start | bytes 49160 | tf_op jit(solution)/shard_map/while/body/eval_jaxpr/ppermute | solution.py:20
  102.7 1.3 collective-permute-start.1
  105.8 3.6 multiply_add_fusion.6
  110.3 4.8 %collective-permute-start = (f32[1,1,16,256]{3,2,1,0:T(8,128)S(1)}, f32[1,1,16,256]{3,2,1,0:T(8,128)S(1)}, u32[]{:S(2)}, u32[]{:S(2)}) collective-permute-start(f32[1,1,16,256]{3,2,1,0:T(8,128)S(1)} %get-tuple-element.979), channel_id=1, source_target_pairs={{0,1},{1,2},{2,3},{3,4},{4,5},{5,6},{6,7},{8,9},{9,10},{10,11},{11... | collective-permute-start | bytes 49160 | tf_op jit(solution)/shard_map/while/body/eval_jaxpr/ppermute | solution.py:20
  115.2 1.3 collective-permute-start.1
  118.2 3.6 multiply_add_fusion.6
  122.9 4.8 %collective-permute-start.8 = (f32[1,1,16,256]{3,2,1,0:T(8,128)S(1)}, f32[1,1,16,256]{3,2,1,0:T(8,128)S(1)}, u32[]{:S(2)}, u32[]{:S(2)}) collective-permute-start(f32[1,1,16,256]{3,2,1,0:T(8,128)S(1)} %get-tuple-element.831), channel_id=1, source_target_pairs={{0,1},{1,2},{2,3},{3,4},{4,5},{5,6},{6,7},{8,9},{9,10},{10,11},{11... | collective-permute-start | bytes 49160 | tf_op jit(solution)/shard_map/ppermute | solution.py:20
  127.7 1.3 collective-permute-start.9
  130.1 1.7 add.631
  131.9 1.4 broadcast_multiply_fusion.10
  133.3 4.0 broadcast_multiply_fusion.5
  137.3 76.5 %while.64 = (s32[]{:T(128)}, f32[8,16,16,256]{3,2,1,0:T(8,128)}, f32[8,16,16,256]{3,2,1,0:T(8,128)}, f32[8,16,16,256]{3,2,1,0:T(8,128)}, f32[16,16,256]{2,1,0:T(...) while((s32[]{:T(128)}, f32[8,16,16,256]{3,2,1,0:T(8,128)}, ...), condition=%wide.region_4.5_spmd.clone.clone, body=%wide.region_3.4_spmd.sunk.clone.clone.sunk | while | flops 14811139 | bytes 23068904 | solution.py:133
  137.3 1.6 copy.50
  139.6 4.5 %collective-permute-start.2 = (f32[8,1,16,256]{3,2,1,0:T(8,128)}, f32[8,1,16,256]{3,2,1,0:T(8,128)}, u32[]{:S(2)}, u32[]{:S(2)}) collective-permute-start(f32[8,1,16,256]{3,2,1,0:T(8,128)} %get-tuple-element.995), channel_id=1, source_target_pairs={{0,1},{1,2},{2,3},{3,4},{4,5},{5,6},{6,7},{8,9},{9,10},{10,11},{11... | collective-permute-start | bytes 393224 | tf_op jit(solution)/shard_map/while/body/eval_jaxpr/ppermute | solution.py:20
  144.0 1.3 collective-permute-start.3
  147.8 7.1 %multiply_add_fusion.7 = (f32[8,16,16,256]{3,2,1,0:T(8,128)}, f32[8,16,16,256]{3,2,1,0:T(8,128)}, f32[8,16,16,256]{3,2,1,0:T(8,128)}) fusion(f32[8,16,16,256]{3,2,1,0:T(8,128)S(1)} %copy.50, f32[]{:T(128)} %bitcast.98, f32[]{:T(128)} %bitcast.99, f32[8,16,16,256]{3,2,1,0:T(8,128)} %get-tuple-element.1066, f32[16,16,256]{2,1,0:T(8,128)S(1)} %get-tuple-element.991, ...), kind=kLoop, calls=%fused_computation.69.clone.1 | loop fusion | flops 14155776 | bytes 14417929 | tf_op jit(solution)/shard_map/while/body/eval_jaxpr/add | solution.py:130
  154.9 1.6 copy.50
  157.3 6.1 %collective-permute-start.2 = (f32[8,1,16,256]{3,2,1,0:T(8,128)}, f32[8,1,16,256]{3,2,1,0:T(8,128)}, u32[]{:S(2)}, u32[]{:S(2)}) collective-permute-start(f32[8,1,16,256]{3,2,1,0:T(8,128)} %get-tuple-element.995), channel_id=1, source_target_pairs={{0,1},{1,2},{2,3},{3,4},{4,5},{5,6},{6,7},{8,9},{9,10},{10,11},{11... | collective-permute-start | bytes 393224 | tf_op jit(solution)/shard_map/while/body/eval_jaxpr/ppermute | solution.py:20
  163.3 1.3 collective-permute-start.3
  167.0 7.5 %multiply_add_fusion.7 = (f32[8,16,16,256]{3,2,1,0:T(8,128)}, f32[8,16,16,256]{3,2,1,0:T(8,128)}, f32[8,16,16,256]{3,2,1,0:T(8,128)}) fusion(f32[8,16,16,256]{3,2,1,0:T(8,128)S(1)} %copy.50, f32[]{:T(128)} %bitcast.98, f32[]{:T(128)} %bitcast.99, f32[8,16,16,256]{3,2,1,0:T(8,128)} %get-tuple-element.1066, f32[16,16,256]{2,1,0:T(8,128)S(1)} %get-tuple-element.991, ...), kind=kLoop, calls=%fused_computation.69.clone.1 | loop fusion | flops 14155776 | bytes 14417929 | tf_op jit(solution)/shard_map/while/body/eval_jaxpr/add | solution.py:130
  174.4 1.6 copy.50
  176.7 6.7 %collective-permute-start.2 = (f32[8,1,16,256]{3,2,1,0:T(8,128)}, f32[8,1,16,256]{3,2,1,0:T(8,128)}, u32[]{:S(2)}, u32[]{:S(2)}) collective-permute-start(f32[8,1,16,256]{3,2,1,0:T(8,128)} %get-tuple-element.995), channel_id=1, source_target_pairs={{0,1},{1,2},{2,3},{3,4},{4,5},{5,6},{6,7},{8,9},{9,10},{10,11},{11... | collective-permute-start | bytes 393224 | tf_op jit(solution)/shard_map/while/body/eval_jaxpr/ppermute | solution.py:20
  183.4 1.3 collective-permute-start.3
  187.1 7.5 %multiply_add_fusion.7 = (f32[8,16,16,256]{3,2,1,0:T(8,128)}, f32[8,16,16,256]{3,2,1,0:T(8,128)}, f32[8,16,16,256]{3,2,1,0:T(8,128)}) fusion(f32[8,16,16,256]{3,2,1,0:T(8,128)S(1)} %copy.50, f32[]{:T(128)} %bitcast.98, f32[]{:T(128)} %bitcast.99, f32[8,16,16,256]{3,2,1,0:T(8,128)} %get-tuple-element.1066, f32[16,16,256]{2,1,0:T(8,128)S(1)} %get-tuple-element.991, ...), kind=kLoop, calls=%fused_computation.69.clone.1 | loop fusion | flops 14155776 | bytes 14417929 | tf_op jit(solution)/shard_map/while/body/eval_jaxpr/add | solution.py:130
  194.5 1.6 copy.50
  196.8 5.8 %collective-permute-start.2 = (f32[8,1,16,256]{3,2,1,0:T(8,128)}, f32[8,1,16,256]{3,2,1,0:T(8,128)}, u32[]{:S(2)}, u32[]{:S(2)}) collective-permute-start(f32[8,1,16,256]{3,2,1,0:T(8,128)} %get-tuple-element.995), channel_id=1, source_target_pairs={{0,1},{1,2},{2,3},{3,4},{4,5},{5,6},{6,7},{8,9},{9,10},{10,11},{11... | collective-permute-start | bytes 393224 | tf_op jit(solution)/shard_map/while/body/eval_jaxpr/ppermute | solution.py:20
  202.6 1.3 collective-permute-start.3
  206.3 7.5 %multiply_add_fusion.7 = (f32[8,16,16,256]{3,2,1,0:T(8,128)}, f32[8,16,16,256]{3,2,1,0:T(8,128)}, f32[8,16,16,256]{3,2,1,0:T(8,128)}) fusion(f32[8,16,16,256]{3,2,1,0:T(8,128)S(1)} %copy.50, f32[]{:T(128)} %bitcast.98, f32[]{:T(128)} %bitcast.99, f32[8,16,16,256]{3,2,1,0:T(8,128)} %get-tuple-element.1066, f32[16,16,256]{2,1,0:T(8,128)S(1)} %get-tuple-element.991, ...), kind=kLoop, calls=%fused_computation.69.clone.1 | loop fusion | flops 14155776 | bytes 14417929 | tf_op jit(solution)/shard_map/while/body/eval_jaxpr/add | solution.py:130
  213.7 4.9 %broadcast_multiply_fusion.4 = (f32[8,16,16,256]{3,2,1,0:T(8,128)}, f32[8,16,16,256]{3,2,1,0:T(8,128)}) fusion(f32[16,16,256]{2,1,0:T(8,128)} %add.631, f32[8,16,16,256]{3,2,1,0:T(8,128)} %get-tuple-element.571, f32[8,16,16,256]{3,2,1,0:T(8,128)} %get-tuple-element.572), kind=kLoop, calls=%fused_computation.180 | loop fusion | flops 1572864 | bytes 8650752 | tf_op jit(solution)/shard_map/mul | solution.py:122
  218.7 75.9 %while.65 = (s32[]{:T(128)}, f32[8,16,16,256]{3,2,1,0:T(8,128)}, f32[8,16,16,256]{3,2,1,0:T(8,128)}, f32[8,16,16,256]{3,2,1,0:T(8,128)}, f32[16,16,256]{2,1,0:T(...) while((s32[]{:T(128)}, f32[8,16,16,256]{3,2,1,0:T(8,128)}, ...), condition=%wide.region_7.8_spmd.clone.clone, body=%wide.region_6.7_spmd.sunk.clone.clone.sunk | while | flops 14811139 | bytes 23068904 | solution.py:133
  218.7 1.6 copy.51
  221.0 5.8 %collective-permute-start.4 = (f32[8,1,16,256]{3,2,1,0:T(8,128)}, f32[8,1,16,256]{3,2,1,0:T(8,128)}, u32[]{:S(2)}, u32[]{:S(2)}) collective-permute-start(f32[8,1,16,256]{3,2,1,0:T(8,128)} %get-tuple-element.1013), channel_id=1, source_target_pairs={{0,1},{1,2},{2,3},{3,4},{4,5},{5,6},{6,7},{8,9},{9,10},{10,11},{11... | collective-permute-start | bytes 393224 | tf_op jit(solution)/shard_map/while/body/eval_jaxpr/ppermute | solution.py:20
  230.3 7.0 %multiply_add_fusion.8 = (f32[8,16,16,256]{3,2,1,0:T(8,128)}, f32[8,16,16,256]{3,2,1,0:T(8,128)}, f32[8,16,16,256]{3,2,1,0:T(8,128)}) fusion(f32[8,16,16,256]{3,2,1,0:T(8,128)S(1)} %copy.51, f32[]{:T(128)} %bitcast.100, f32[]{:T(128)} %bitcast.101, f32[8,16,16,256]{3,2,1,0:T(8,128)} %get-tuple-element.1099, ...), kind=kLoop, calls=%fused_computation.110.clone.1 | loop fusion | flops 14155776 | bytes 14417929 | tf_op jit(solution)/shard_map/while/body/eval_jaxpr/add | solution.py:130
  237.3 1.6 copy.51
  239.6 5.8 %collective-permute-start.4 = (f32[8,1,16,256]{3,2,1,0:T(8,128)}, f32[8,1,16,256]{3,2,1,0:T(8,128)}, u32[]{:S(2)}, u32[]{:S(2)}) collective-permute-start(f32[8,1,16,256]{3,2,1,0:T(8,128)} %get-tuple-element.1013), channel_id=1, source_target_pairs={{0,1},{1,2},{2,3},{3,4},{4,5},{5,6},{6,7},{8,9},{9,10},{10,11},{11... | collective-permute-start | bytes 393224 | tf_op jit(solution)/shard_map/while/body/eval_jaxpr/ppermute | solution.py:20
  249.1 7.3 %multiply_add_fusion.8 = (f32[8,16,16,256]{3,2,1,0:T(8,128)}, f32[8,16,16,256]{3,2,1,0:T(8,128)}, f32[8,16,16,256]{3,2,1,0:T(8,128)}) fusion(f32[8,16,16,256]{3,2,1,0:T(8,128)S(1)} %copy.51, f32[]{:T(128)} %bitcast.100, f32[]{:T(128)} %bitcast.101, f32[8,16,16,256]{3,2,1,0:T(8,128)} %get-tuple-element.1099, ...), kind=kLoop, calls=%fused_computation.110.clone.1 | loop fusion | flops 14155776 | bytes 14417929 | tf_op jit(solution)/shard_map/while/body/eval_jaxpr/add | solution.py:130
  256.4 1.6 copy.51
  258.7 5.8 %collective-permute-start.4 = (f32[8,1,16,256]{3,2,1,0:T(8,128)}, f32[8,1,16,256]{3,2,1,0:T(8,128)}, u32[]{:S(2)}, u32[]{:S(2)}) collective-permute-start(f32[8,1,16,256]{3,2,1,0:T(8,128)} %get-tuple-element.1013), channel_id=1, source_target_pairs={{0,1},{1,2},{2,3},{3,4},{4,5},{5,6},{6,7},{8,9},{9,10},{10,11},{11... | collective-permute-start | bytes 393224 | tf_op jit(solution)/shard_map/while/body/eval_jaxpr/ppermute | solution.py:20
  268.1 7.3 %multiply_add_fusion.8 = (f32[8,16,16,256]{3,2,1,0:T(8,128)}, f32[8,16,16,256]{3,2,1,0:T(8,128)}, f32[8,16,16,256]{3,2,1,0:T(8,128)}) fusion(f32[8,16,16,256]{3,2,1,0:T(8,128)S(1)} %copy.51, f32[]{:T(128)} %bitcast.100, f32[]{:T(128)} %bitcast.101, f32[8,16,16,256]{3,2,1,0:T(8,128)} %get-tuple-element.1099, ...), kind=kLoop, calls=%fused_computation.110.clone.1 | loop fusion | flops 14155776 | bytes 14417929 | tf_op jit(solution)/shard_map/while/body/eval_jaxpr/add | solution.py:130
  275.5 1.6 copy.51
  277.8 5.8 %collective-permute-start.4 = (f32[8,1,16,256]{3,2,1,0:T(8,128)}, f32[8,1,16,256]{3,2,1,0:T(8,128)}, u32[]{:S(2)}, u32[]{:S(2)}) collective-permute-start(f32[8,1,16,256]{3,2,1,0:T(8,128)} %get-tuple-element.1013), channel_id=1, source_target_pairs={{0,1},{1,2},{2,3},{3,4},{4,5},{5,6},{6,7},{8,9},{9,10},{10,11},{11... | collective-permute-start | bytes 393224 | tf_op jit(solution)/shard_map/while/body/eval_jaxpr/ppermute | solution.py:20
  287.2 7.3 %multiply_add_fusion.8 = (f32[8,16,16,256]{3,2,1,0:T(8,128)}, f32[8,16,16,256]{3,2,1,0:T(8,128)}, f32[8,16,16,256]{3,2,1,0:T(8,128)}) fusion(f32[8,16,16,256]{3,2,1,0:T(8,128)S(1)} %copy.51, f32[]{:T(128)} %bitcast.100, f32[]{:T(128)} %bitcast.101, f32[8,16,16,256]{3,2,1,0:T(8,128)} %get-tuple-element.1099, ...), kind=kLoop, calls=%fused_computation.110.clone.1 | loop fusion | flops 14155776 | bytes 14417929 | tf_op jit(solution)/shard_map/while/body/eval_jaxpr/add | solution.py:130
  294.5 2.7 add.632
  297.3 5.2 %collective-permute-start.10 = (f32[8,1,16,256]{3,2,1,0:T(8,128)S(1)}, f32[8,1,16,256]{3,2,1,0:T(8,128)S(1)}, u32[]{:S(2)}, u32[]{:S(2)}) collective-permute-start(f32[8,1,16,256]{3,2,1,0:T(8,128)S(1)} %get-tuple-element.818), channel_id=1, source_target_pairs={{0,1},{1,2},{2,3},{3,4},{4,5},{5,6},{6,7},{8,9},{9,10},{10,11},{11... | collective-permute-start | bytes 393224 | tf_op jit(solution)/shard_map/ppermute | solution.py:20
  302.5 1.3 collective-permute-start.11
  303.8 1.9 collective-permute-done.11
  307.5 3.2 fusion.107
  310.7 89.1 %all-reduce.20.cloned.1.call-done = f32[8,16,16,256]{3,2,1,0:T(8,128)} async-done(((f32[8,16,16,256]{3,2,1,0:T(8,128)}), f32[8,16,16,256]{3,2,1,0:T(8,128)}) %all-reduce.20.cloned.1.call-update) | async-done | bytes 2097168 | tf_op jit(solution)/shard_map/psum | solution.py:150
  399.8 1.9 constant_dynamic-slice_fusion
  (154 shorter events, 48.2 us)
Async XLA Ops:
  6.5 50.8 %all-gather.2.cloned.1.call-start = ((), (), s32[]{:S(2)}) async-start(), calls=%async_computation | async-start | bytes 2621440 | tf_op jit(solution)/shard_map/all_gather | solution.py:102
  7.3 392.5 %all-reduce.20.cloned.1.call-start = ((), (), s32[]{:S(2)}) async-start(), calls=%async_computation.1 | async-start | bytes 4194304 | tf_op jit(solution)/shard_map/psum | solution.py:150
  9.0 60.8 %copy-start = (f32[1,16,16,256]{3,2,1,0:T(8,128)}, f32[1,16,16,256]{3,2,1,0:T(8,128)S(1)}, u32[]{:S(2)}) copy-start(f32[1,16,16,256]{3,2,1,0:T(8,128)S(1)} %get-tuple-element.823) | copy-start | bytes 786436
  59.3 5.2 %copy-start.13 = (s32[1,8]{1,0:T(1,128)S(1)}, s32[1,8]{1,0:T(1,128)}, u32[]{:S(2)}) copy-start(s32[1,8]{1,0:T(1,128)} %param.16) | copy-start | bytes 100
  59.3 5.2 %copy-start.14 = (f32[1,8]{1,0:T(1,128)S(1)}, f32[1,8]{1,0:T(1,128)}, u32[]{:S(2)}) copy-start(f32[1,8]{1,0:T(1,128)} %param.17) | copy-start | bytes 100
  60.2 7.9 %collective-permute-start.6 = (f32[9,2,16,256]{3,2,1,0:T(8,128)}, f32[9,2,16,256]{3,2,1,0:T(8,128)S(1)}, u32[]{:S(2)}, u32[]{:S(2)}) collective-permute-start(f32[9,2,16,256]{3,2,1,0:T(8,128)} %get-tuple-element.817), channel_id=1, source_target_pairs={{1,0},{2,1},{3,2},{4,3},{5,4},{6,5},{7,6},{9,8},{10,9},{11,10},{12... | collective-permute-start | bytes 884744 | tf_op jit(solution)/shard_map/ppermute | solution.py:22
  61.4 6.7 %collective-permute-start.7 = (f32[9,2,16,256]{3,2,1,0:T(8,128)}, f32[9,2,16,256]{3,2,1,0:T(8,128)S(1)}, u32[]{:S(2)}, u32[]{:S(2)}) collective-permute-start(f32[9,2,16,256]{3,2,1,0:T(8,128)} %get-tuple-element.816), channel_id=1, source_target_pairs={{0,1},{1,2},{2,3},{3,4},{4,5},{5,6},{6,7},{8,9},{9,10},{10,11},{11... | collective-permute-start | bytes 884744 | tf_op jit(solution)/shard_map/ppermute | solution.py:20
  68.1 2.6 copy-start.2
  68.1 0.8 copy-start.4
  69.9 0.8 copy-start.15
  69.9 0.8 copy-start.16
  71.7 5.9 %collective-permute-start = (f32[1,1,16,256]{3,2,1,0:T(8,128)S(1)}, f32[1,1,16,256]{3,2,1,0:T(8,128)S(1)}, u32[]{:S(2)}, u32[]{:S(2)}) collective-permute-start(f32[1,1,16,256]{3,2,1,0:T(8,128)S(1)} %get-tuple-element.979), channel_id=1, source_target_pairs={{0,1},{1,2},{2,3},{3,4},{4,5},{5,6},{6,7},{8,9},{9,10},{10,11},{11... | collective-permute-start | bytes 49160 | tf_op jit(solution)/shard_map/while/body/eval_jaxpr/ppermute | solution.py:20
  75.0 5.0 %collective-permute-start.1 = (f32[1,1,16,256]{3,2,1,0:T(8,128)S(1)}, f32[1,1,16,256]{3,2,1,0:T(8,128)S(1)}, u32[]{:S(2)}, u32[]{:S(2)}) collective-permute-start(f32[1,1,16,256]{3,2,1,0:T(8,128)S(1)} %get-tuple-element.980), channel_id=1, source_target_pairs={{1,0},{2,1},{3,2},{4,3},{5,4},{6,5},{7,6},{9,8},{10,9},{11,10},{12... | collective-permute-start | bytes 49160 | tf_op jit(solution)/shard_map/while/body/eval_jaxpr/ppermute | solution.py:22
  84.4 7.0 %collective-permute-start = (f32[1,1,16,256]{3,2,1,0:T(8,128)S(1)}, f32[1,1,16,256]{3,2,1,0:T(8,128)S(1)}, u32[]{:S(2)}, u32[]{:S(2)}) collective-permute-start(f32[1,1,16,256]{3,2,1,0:T(8,128)S(1)} %get-tuple-element.979), channel_id=1, source_target_pairs={{0,1},{1,2},{2,3},{3,4},{4,5},{5,6},{6,7},{8,9},{9,10},{10,11},{11... | collective-permute-start | bytes 49160 | tf_op jit(solution)/shard_map/while/body/eval_jaxpr/ppermute | solution.py:20
  88.8 3.3 collective-permute-start.1
  96.7 8.6 %collective-permute-start = (f32[1,1,16,256]{3,2,1,0:T(8,128)S(1)}, f32[1,1,16,256]{3,2,1,0:T(8,128)S(1)}, u32[]{:S(2)}, u32[]{:S(2)}) collective-permute-start(f32[1,1,16,256]{3,2,1,0:T(8,128)S(1)} %get-tuple-element.979), channel_id=1, source_target_pairs={{0,1},{1,2},{2,3},{3,4},{4,5},{5,6},{6,7},{8,9},{9,10},{10,11},{11... | collective-permute-start | bytes 49160 | tf_op jit(solution)/shard_map/while/body/eval_jaxpr/ppermute | solution.py:20
  102.7 3.1 collective-permute-start.1
  110.3 7.4 %collective-permute-start = (f32[1,1,16,256]{3,2,1,0:T(8,128)S(1)}, f32[1,1,16,256]{3,2,1,0:T(8,128)S(1)}, u32[]{:S(2)}, u32[]{:S(2)}) collective-permute-start(f32[1,1,16,256]{3,2,1,0:T(8,128)S(1)} %get-tuple-element.979), channel_id=1, source_target_pairs={{0,1},{1,2},{2,3},{3,4},{4,5},{5,6},{6,7},{8,9},{9,10},{10,11},{11... | collective-permute-start | bytes 49160 | tf_op jit(solution)/shard_map/while/body/eval_jaxpr/ppermute | solution.py:20
  115.2 3.1 collective-permute-start.1
  122.9 8.9 %collective-permute-start.8 = (f32[1,1,16,256]{3,2,1,0:T(8,128)S(1)}, f32[1,1,16,256]{3,2,1,0:T(8,128)S(1)}, u32[]{:S(2)}, u32[]{:S(2)}) collective-permute-start(f32[1,1,16,256]{3,2,1,0:T(8,128)S(1)} %get-tuple-element.831), channel_id=1, source_target_pairs={{0,1},{1,2},{2,3},{3,4},{4,5},{5,6},{6,7},{8,9},{9,10},{10,11},{11... | collective-permute-start | bytes 49160 | tf_op jit(solution)/shard_map/ppermute | solution.py:20
  127.7 4.1 collective-permute-start.9
  131.9 1.4 copy-start.1
  131.9 1.4 copy-start.3
  131.9 1.4 copy-start.5
  139.6 8.1 %collective-permute-start.2 = (f32[8,1,16,256]{3,2,1,0:T(8,128)}, f32[8,1,16,256]{3,2,1,0:T(8,128)}, u32[]{:S(2)}, u32[]{:S(2)}) collective-permute-start(f32[8,1,16,256]{3,2,1,0:T(8,128)} %get-tuple-element.995), channel_id=1, source_target_pairs={{0,1},{1,2},{2,3},{3,4},{4,5},{5,6},{6,7},{8,9},{9,10},{10,11},{11... | collective-permute-start | bytes 393224 | tf_op jit(solution)/shard_map/while/body/eval_jaxpr/ppermute | solution.py:20
  144.0 3.8 collective-permute-start.3
  157.3 9.7 %collective-permute-start.2 = (f32[8,1,16,256]{3,2,1,0:T(8,128)}, f32[8,1,16,256]{3,2,1,0:T(8,128)}, u32[]{:S(2)}, u32[]{:S(2)}) collective-permute-start(f32[8,1,16,256]{3,2,1,0:T(8,128)} %get-tuple-element.995), channel_id=1, source_target_pairs={{0,1},{1,2},{2,3},{3,4},{4,5},{5,6},{6,7},{8,9},{9,10},{10,11},{11... | collective-permute-start | bytes 393224 | tf_op jit(solution)/shard_map/while/body/eval_jaxpr/ppermute | solution.py:20
  163.3 3.6 collective-permute-start.3
  176.7 10.3 %collective-permute-start.2 = (f32[8,1,16,256]{3,2,1,0:T(8,128)}, f32[8,1,16,256]{3,2,1,0:T(8,128)}, u32[]{:S(2)}, u32[]{:S(2)}) collective-permute-start(f32[8,1,16,256]{3,2,1,0:T(8,128)} %get-tuple-element.995), channel_id=1, source_target_pairs={{0,1},{1,2},{2,3},{3,4},{4,5},{5,6},{6,7},{8,9},{9,10},{10,11},{11... | collective-permute-start | bytes 393224 | tf_op jit(solution)/shard_map/while/body/eval_jaxpr/ppermute | solution.py:20
  183.4 3.6 collective-permute-start.3
  196.8 9.4 %collective-permute-start.2 = (f32[8,1,16,256]{3,2,1,0:T(8,128)}, f32[8,1,16,256]{3,2,1,0:T(8,128)}, u32[]{:S(2)}, u32[]{:S(2)}) collective-permute-start(f32[8,1,16,256]{3,2,1,0:T(8,128)} %get-tuple-element.995), channel_id=1, source_target_pairs={{0,1},{1,2},{2,3},{3,4},{4,5},{5,6},{6,7},{8,9},{9,10},{10,11},{11... | collective-permute-start | bytes 393224 | tf_op jit(solution)/shard_map/while/body/eval_jaxpr/ppermute | solution.py:20
  202.6 3.6 collective-permute-start.3
  221.0 9.3 %collective-permute-start.4 = (f32[8,1,16,256]{3,2,1,0:T(8,128)}, f32[8,1,16,256]{3,2,1,0:T(8,128)}, u32[]{:S(2)}, u32[]{:S(2)}) collective-permute-start(f32[8,1,16,256]{3,2,1,0:T(8,128)} %get-tuple-element.1013), channel_id=1, source_target_pairs={{0,1},{1,2},{2,3},{3,4},{4,5},{5,6},{6,7},{8,9},{9,10},{10,11},{11... | collective-permute-start | bytes 393224 | tf_op jit(solution)/shard_map/while/body/eval_jaxpr/ppermute | solution.py:20
  226.8 3.6 collective-permute-start.5
  239.6 9.4 %collective-permute-start.4 = (f32[8,1,16,256]{3,2,1,0:T(8,128)}, f32[8,1,16,256]{3,2,1,0:T(8,128)}, u32[]{:S(2)}, u32[]{:S(2)}) collective-permute-start(f32[8,1,16,256]{3,2,1,0:T(8,128)} %get-tuple-element.1013), channel_id=1, source_target_pairs={{0,1},{1,2},{2,3},{3,4},{4,5},{5,6},{6,7},{8,9},{9,10},{10,11},{11... | collective-permute-start | bytes 393224 | tf_op jit(solution)/shard_map/while/body/eval_jaxpr/ppermute | solution.py:20
  245.5 3.6 collective-permute-start.5
  258.7 9.4 %collective-permute-start.4 = (f32[8,1,16,256]{3,2,1,0:T(8,128)}, f32[8,1,16,256]{3,2,1,0:T(8,128)}, u32[]{:S(2)}, u32[]{:S(2)}) collective-permute-start(f32[8,1,16,256]{3,2,1,0:T(8,128)} %get-tuple-element.1013), channel_id=1, source_target_pairs={{0,1},{1,2},{2,3},{3,4},{4,5},{5,6},{6,7},{8,9},{9,10},{10,11},{11... | collective-permute-start | bytes 393224 | tf_op jit(solution)/shard_map/while/body/eval_jaxpr/ppermute | solution.py:20
  264.6 3.6 collective-permute-start.5
  277.8 9.4 %collective-permute-start.4 = (f32[8,1,16,256]{3,2,1,0:T(8,128)}, f32[8,1,16,256]{3,2,1,0:T(8,128)}, u32[]{:S(2)}, u32[]{:S(2)}) collective-permute-start(f32[8,1,16,256]{3,2,1,0:T(8,128)} %get-tuple-element.1013), channel_id=1, source_target_pairs={{0,1},{1,2},{2,3},{3,4},{4,5},{5,6},{6,7},{8,9},{9,10},{10,11},{11... | collective-permute-start | bytes 393224 | tf_op jit(solution)/shard_map/while/body/eval_jaxpr/ppermute | solution.py:20
  283.6 3.6 collective-permute-start.5
  297.3 6.5 %collective-permute-start.10 = (f32[8,1,16,256]{3,2,1,0:T(8,128)S(1)}, f32[8,1,16,256]{3,2,1,0:T(8,128)S(1)}, u32[]{:S(2)}, u32[]{:S(2)}) collective-permute-start(f32[8,1,16,256]{3,2,1,0:T(8,128)S(1)} %get-tuple-element.818), channel_id=1, source_target_pairs={{0,1},{1,2},{2,3},{3,4},{4,5},{5,6},{6,7},{8,9},{9,10},{10,11},{11... | collective-permute-start | bytes 393224 | tf_op jit(solution)/shard_map/ppermute | solution.py:20
  302.5 3.2 collective-permute-start.11
  306.1 1.0 copy-start.6
  306.1 1.0 copy-start.7
  306.1 1.1 copy-start.8
  306.1 1.2 copy-start.9
  306.1 1.2 copy-start.10
  306.1 1.3 copy-start.11
  306.1 1.4 copy-start.12
Sparse Core Ops, SparseCore 0:
  8.9 48.3 all-gather.1
  310.8 88.8 all-reduce.19
where the time goes:
time: 410 us; the launch traced here: 408 us
  waiting for transfers between devices  144 us (35%)
  other arithmetic  110 us (27%)
  starting transfers between devices  97.2 us (24%)
  local copies, waits for them, and re-layouts  42.9 us (10%)
  between operations  13.8 us (3%)
    psum x1, waiting for transfers between devices, shards(): total = lax.psum(partial_value, 'test')  89.1 us
    ppermute x15, starting transfers between devices, with_halo(): lax.ppermute(tail, axis, [(i, (i + 1) % count) for i in range(ends)])  77.9 us
    add x12, other arithmetic, sweep(): direction = keep_table[turn] * direction + push_table[turn] * residual  72.8 us
    all_gather x1, waiting for transfers between devices, shards(): columns = lax.all_gather(panel, 'test', axis=0, tiled=True)  48.2 us
    ppermute x15, starting transfers between devices, with_halo(): lax.ppermute(head, axis, [((i + 1) % count, i) for i in range(ends)])  19.3 us
    while x12, local copies, waits for them, and re-layouts  16.5 us
    dynamic_slice x24, local copies, waits for them, and re-layouts, sweep(): direction = keep_table[turn] * direction + push_table[turn] * residual  15.1 us
    mul x3, other arithmetic, solve(): direction = right_side * first  10.7 us
  transfers between devices with their start and end apart: 32, of which 8 were waited for; matrix products, arithmetic and copies ran while one was open for 8% of the time, Pallas kernels for 0%

commit v1 on v0

--- a/solution.py
+++ b/solution.py
@@ -7,6 +7,13 @@
 
 CHEB = 4
 storage = 0.02
+
+
+def store_spots(local_x, axis_k):
+    new = list(local_x.shape[1:])
+    new[axis_k] *= local_x.shape[0]
+    k_now = jnp.moveaxis(local_x, 0, axis_k).reshape(new)
+    return k_now
 
 
 def with_halo(cells, sides, width):
@@ -99,7 +106,36 @@
     first, keeps, pushes = cheb_table(CHEB)
     keep_table = jnp.asarray(np.array(keeps, np.float32))
     push_table = jnp.asarray(np.array(pushes, np.float32))
-    columns = lax.all_gather(panel, "test", axis=0, tiled=True)
+
+    def plan_the_chunk(out_dim, mesh_ax, block_here):
+        axis_n = jax.lax.psum(1, axis_name=mesh_ax)
+        series = []
+        for src_i in range(axis_n):
+            series.append((src_i, (src_i + 1) % axis_n))
+        parts_seen = []
+        for c, jj in series:
+            parts_seen.append((jj, c))
+        now, piece_next = ([], [])
+        for ii in range(axis_n - 1):
+            if ii % 2 == 0:
+                now.append(
+                    jax.lax.ppermute(now[-1] if now else block_here, axis_name=mesh_ax, perm=series)
+                )
+            else:
+                piece_next.append(
+                    jax.lax.ppermute(
+                        piece_next[-1] if piece_next else block_here,
+                        axis_name=mesh_ax,
+                        perm=parts_seen,
+                    )
+                )
+        y2 = jnp.stack([*now[::-1], block_here, *piece_next], axis=0)
+        n_now = jax.lax.axis_index(mesh_ax) - len(now)
+        y2 = y2[(jnp.arange(axis_n) - n_now) % axis_n]
+        upper = store_spots(y2, out_dim)
+        return upper
+
+    columns = plan_the_chunk(0, "test", panel)
     columns_all = columns.shape[0]
     perm = jnp.exp(log_perm)
     stacked = jnp.concatenate([perm[None], perm[None] * columns], axis=0)

time: 410 us -> 404 us (0.985)
  waiting for transfers between devices: 144 us -> 127 us
  starting transfers between devices: 97.2 us -> 103 us
    all_gather x1 -> x0, waiting for transfers between devices: 48.2 us -> none  [shards(): columns = lax.all_gather(panel, 'test', axis=0, tiled=True)]
    ppermute x0 -> x3, waiting for transfers between devices: none -> 32.7 us  [the longest x2 24.6 us: plan_the_chunk(): jax.lax.ppermute(now[-1] if now else block_here, axis_name=mesh_ax, perm=...]
    ppermute x0 -> x3, starting transfers between devices: none -> 5.08 us  [the longest x2 3.05 us: plan_the_chunk(): jax.lax.ppermute(now[-1] if now else block_here, axis_name=mesh_ax, perm=...]
  transfers between devices with their start and end apart: 32 -> 34, of which waited for: 8 -> 11; matrix products, arithmetic and copies ran while one was open for 8% -> 8% of each run, Pallas kernels for 0% -> 0%
where the time goes in v1:
time: 404 us; the launch traced here: 402 us
  waiting for transfers between devices  127 us (31%)
  other arithmetic  112 us (28%)
  starting transfers between devices  103 us (25%)
  local copies, waits for them, and re-layouts  45.7 us (11%)
  between operations  13.8 us (3%)
    psum x1, waiting for transfers between devices, shards(): total = lax.psum(partial_value, 'test')  89.3 us
    ppermute x15, starting transfers between devices, with_halo(): lax.ppermute(tail, axis, [(i, (i + 1) % count) for i in range(ends)])  78.7 us
    add x12, other arithmetic, sweep(): direction = keep_table[turn] * direction + push_table[turn] * residual  72.7 us
    ppermute x2, waiting for transfers between devices, plan_the_chunk(): jax.lax.ppermute(now[-1] if now else block_here, axis_name=mesh_ax, perm=...  24.6 us
    ppermute x15, starting transfers between devices, with_halo(): lax.ppermute(head, axis, [((i + 1) % count, i) for i in range(ends)])  19.3 us
    while x12, local copies, waits for them, and re-layouts  16.5 us
    dynamic_slice x24, local copies, waits for them, and re-layouts, sweep(): direction = keep_table[turn] * direction + push_table[turn] * residual  15.2 us
    mul x3, other arithmetic, solve(): direction = right_side * first  10.7 us
  transfers between devices with their start and end apart: 34, of which 11 were waited for; matrix products, arithmetic and copies ran while one was open for 8% of the time, Pallas kernels for 0%

profile of v1, /device:TPU:0, one launch (start us, length us, event | category | flops | bytes accessed | tf_op | source)
XLA Modules:
  0.0 401.6 jit_solution(11002438189142626333)
XLA Ops:
  6.5 3.1 collective-permute-start.6
  9.6 2.0 collective-permute-start.8
  11.6 13.0 %collective-permute-done.6 = f32[2,16,16,256]{3,2,1,0:T(8,128)S(1)} collective-permute-done((f32[2,16,16,256]{3,2,1,0:T(8,128)}, f32[2,16,16,256]{3,2,1,0:T(8,128)S(1)}, u32[]{:S(2)}, u32[]{:S(2)}) %collective-permute-start.6) | collective-permute-done | bytes 524320 | tf_op jit(solution)/shard_map/ppermute | solution.py:122
  24.7 1.9 broadcast_multiply_fusion.13
  26.6 8.1 %collective-permute-done.8 = f32[2,16,16,256]{3,2,1,0:T(8,128)S(1)} collective-permute-done((f32[2,16,16,256]{3,2,1,0:T(8,128)}, f32[2,16,16,256]{3,2,1,0:T(8,128)S(1)}, u32[]{:S(2)}, u32[]{:S(2)}) %collective-permute-start.8) | collective-permute-done | bytes 524320 | tf_op jit(solution)/shard_map/ppermute | solution.py:126
  34.7 11.6 %collective-permute-done.7 = f32[2,16,16,256]{3,2,1,0:T(8,128)S(1)} collective-permute-done((f32[2,16,16,256]{3,2,1,0:T(8,128)S(1)}, f32[2,16,16,256]{3,2,1,0:T(8,128)S(1)}, u32[]{:S(2)}, u32[]{:S(2)}) %collective-permute-start.7) | collective-permute-done | bytes 524320 | tf_op jit(solution)/shard_map/ppermute | solution.py:122
  47.1 1.8 pad_maximum_fusion.10
  48.9 2.0 gather_fusion
  50.9 2.0 bitcast_multiply_fusion
  53.7 1.3 collective-permute-start.10
  55.0 1.3 collective-permute-start.9
  56.4 1.7 fusion.86
  58.1 1.8 broadcast_multiply_fusion.12
  63.0 51.5 %while.63 = (s32[]{:T(128)}, f32[1,16,16,256]{3,2,1,0:T(8,128)}, f32[1,16,16,256]{3,2,1,0:T(8,128)}, f32[1,16,16,256]{3,2,1,0:T(8,128)}, f32[16,16,256]{2,1,0:T(...) while((s32[]{:T(128)}, f32[1,16,16,256]{3,2,1,0:T(8,128)}, ...), condition=%wide.region_2.3_spmd.clone.clone, body=%wide.region_1.2_spmd.sunk.clone.clone.sunk | while | flops 2424835 | bytes 3637479 | solution.py:169
  64.0 7.4 %collective-permute-start = (f32[1,1,16,256]{3,2,1,0:T(8,128)S(1)}, f32[1,1,16,256]{3,2,1,0:T(8,128)S(1)}, u32[]{:S(2)}, u32[]{:S(2)}) collective-permute-start(f32[1,1,16,256]{3,2,1,0:T(8,128)S(1)} %get-tuple-element.979), channel_id=1, source_target_pairs={{0,1},{1,2},{2,3},{3,4},{4,5},{5,6},{6,7},{8,9},{9,10},{10,11},{11... | collective-permute-start | bytes 49160 | tf_op jit(solution)/shard_map/while/body/eval_jaxpr/ppermute | solution.py:27
  71.4 1.3 collective-permute-start.1
  74.5 3.5 multiply_add_fusion.6
  78.9 4.2 %collective-permute-start = (f32[1,1,16,256]{3,2,1,0:T(8,128)S(1)}, f32[1,1,16,256]{3,2,1,0:T(8,128)S(1)}, u32[]{:S(2)}, u32[]{:S(2)}) collective-permute-start(f32[1,1,16,256]{3,2,1,0:T(8,128)S(1)} %get-tuple-element.979), channel_id=1, source_target_pairs={{0,1},{1,2},{2,3},{3,4},{4,5},{5,6},{6,7},{8,9},{9,10},{10,11},{11... | collective-permute-start | bytes 49160 | tf_op jit(solution)/shard_map/while/body/eval_jaxpr/ppermute | solution.py:27
  83.1 1.3 collective-permute-start.1
  86.2 3.5 multiply_add_fusion.6
  90.7 4.8 %collective-permute-start = (f32[1,1,16,256]{3,2,1,0:T(8,128)S(1)}, f32[1,1,16,256]{3,2,1,0:T(8,128)S(1)}, u32[]{:S(2)}, u32[]{:S(2)}) collective-permute-start(f32[1,1,16,256]{3,2,1,0:T(8,128)S(1)} %get-tuple-element.979), channel_id=1, source_target_pairs={{0,1},{1,2},{2,3},{3,4},{4,5},{5,6},{6,7},{8,9},{9,10},{10,11},{11... | collective-permute-start | bytes 49160 | tf_op jit(solution)/shard_map/while/body/eval_jaxpr/ppermute | solution.py:27
  95.5 1.3 collective-permute-start.1
  98.6 3.5 multiply_add_fusion.6
  103.1 4.8 %collective-permute-start = (f32[1,1,16,256]{3,2,1,0:T(8,128)S(1)}, f32[1,1,16,256]{3,2,1,0:T(8,128)S(1)}, u32[]{:S(2)}, u32[]{:S(2)}) collective-permute-start(f32[1,1,16,256]{3,2,1,0:T(8,128)S(1)} %get-tuple-element.979), channel_id=1, source_target_pairs={{0,1},{1,2},{2,3},{3,4},{4,5},{5,6},{6,7},{8,9},{9,10},{10,11},{11... | collective-permute-start | bytes 49160 | tf_op jit(solution)/shard_map/while/body/eval_jaxpr/ppermute | solution.py:27
  107.9 1.3 collective-permute-start.1
  110.9 3.5 multiply_add_fusion.6
  115.6 4.8 %collective-permute-start.11 = (f32[1,1,16,256]{3,2,1,0:T(8,128)S(1)}, f32[1,1,16,256]{3,2,1,0:T(8,128)S(1)}, u32[]{:S(2)}, u32[]{:S(2)}) collective-permute-start(f32[1,1,16,256]{3,2,1,0:T(8,128)S(1)} %get-tuple-element.831), channel_id=1, source_target_pairs={{0,1},{1,2},{2,3},{3,4},{4,5},{5,6},{6,7},{8,9},{9,10},{10,11},{11... | collective-permute-start | bytes 49160 | tf_op jit(solution)/shard_map/ppermute | solution.py:27
  120.4 1.3 collective-permute-start.12
  122.7 1.7 add.657
  124.5 1.3 broadcast_multiply_fusion.9
  125.9 4.0 broadcast_multiply_fusion.5
  129.9 76.5 %while.64 = (s32[]{:T(128)}, f32[8,16,16,256]{3,2,1,0:T(8,128)}, f32[8,16,16,256]{3,2,1,0:T(8,128)}, f32[8,16,16,256]{3,2,1,0:T(8,128)}, f32[16,16,256]{2,1,0:T(...) while((s32[]{:T(128)}, f32[8,16,16,256]{3,2,1,0:T(8,128)}, ...), condition=%wide.region_4.5_spmd.clone.clone, body=%wide.region_3.4_spmd.sunk.clone.clone.sunk | while | flops 14811139 | bytes 23068904 | solution.py:169
  129.9 1.6 copy.50
  132.2 4.5 %collective-permute-start.2 = (f32[8,1,16,256]{3,2,1,0:T(8,128)}, f32[8,1,16,256]{3,2,1,0:T(8,128)}, u32[]{:S(2)}, u32[]{:S(2)}) collective-permute-start(f32[8,1,16,256]{3,2,1,0:T(8,128)} %get-tuple-element.995), channel_id=1, source_target_pairs={{0,1},{1,2},{2,3},{3,4},{4,5},{5,6},{6,7},{8,9},{9,10},{10,11},{11... | collective-permute-start | bytes 393224 | tf_op jit(solution)/shard_map/while/body/eval_jaxpr/ppermute | solution.py:27
  140.5 7.1 %multiply_add_fusion.7 = (f32[8,16,16,256]{3,2,1,0:T(8,128)}, f32[8,16,16,256]{3,2,1,0:T(8,128)}, f32[8,16,16,256]{3,2,1,0:T(8,128)}) fusion(f32[8,16,16,256]{3,2,1,0:T(8,128)S(1)} %copy.50, f32[]{:T(128)} %bitcast.106, f32[]{:T(128)} %bitcast.107, f32[8,16,16,256]{3,2,1,0:T(8,128)} %get-tuple-element.1066, ...), kind=kLoop, calls=%fused_computation.70.clone.1 | loop fusion | flops 14155776 | bytes 14417929 | tf_op jit(solution)/shard_map/while/body/eval_jaxpr/add | solution.py:166
  147.6 1.6 copy.50
  149.9 6.1 %collective-permute-start.2 = (f32[8,1,16,256]{3,2,1,0:T(8,128)}, f32[8,1,16,256]{3,2,1,0:T(8,128)}, u32[]{:S(2)}, u32[]{:S(2)}) collective-permute-start(f32[8,1,16,256]{3,2,1,0:T(8,128)} %get-tuple-element.995), channel_id=1, source_target_pairs={{0,1},{1,2},{2,3},{3,4},{4,5},{5,6},{6,7},{8,9},{9,10},{10,11},{11... | collective-permute-start | bytes 393224 | tf_op jit(solution)/shard_map/while/body/eval_jaxpr/ppermute | solution.py:27
  159.6 7.5 %multiply_add_fusion.7 = (f32[8,16,16,256]{3,2,1,0:T(8,128)}, f32[8,16,16,256]{3,2,1,0:T(8,128)}, f32[8,16,16,256]{3,2,1,0:T(8,128)}) fusion(f32[8,16,16,256]{3,2,1,0:T(8,128)S(1)} %copy.50, f32[]{:T(128)} %bitcast.106, f32[]{:T(128)} %bitcast.107, f32[8,16,16,256]{3,2,1,0:T(8,128)} %get-tuple-element.1066, ...), kind=kLoop, calls=%fused_computation.70.clone.1 | loop fusion | flops 14155776 | bytes 14417929 | tf_op jit(solution)/shard_map/while/body/eval_jaxpr/add | solution.py:166
  167.1 1.6 copy.50
  169.4 6.7 %collective-permute-start.2 = (f32[8,1,16,256]{3,2,1,0:T(8,128)}, f32[8,1,16,256]{3,2,1,0:T(8,128)}, u32[]{:S(2)}, u32[]{:S(2)}) collective-permute-start(f32[8,1,16,256]{3,2,1,0:T(8,128)} %get-tuple-element.995), channel_id=1, source_target_pairs={{0,1},{1,2},{2,3},{3,4},{4,5},{5,6},{6,7},{8,9},{9,10},{10,11},{11... | collective-permute-start | bytes 393224 | tf_op jit(solution)/shard_map/while/body/eval_jaxpr/ppermute | solution.py:27
  179.7 7.5 %multiply_add_fusion.7 = (f32[8,16,16,256]{3,2,1,0:T(8,128)}, f32[8,16,16,256]{3,2,1,0:T(8,128)}, f32[8,16,16,256]{3,2,1,0:T(8,128)}) fusion(f32[8,16,16,256]{3,2,1,0:T(8,128)S(1)} %copy.50, f32[]{:T(128)} %bitcast.106, f32[]{:T(128)} %bitcast.107, f32[8,16,16,256]{3,2,1,0:T(8,128)} %get-tuple-element.1066, ...), kind=kLoop, calls=%fused_computation.70.clone.1 | loop fusion | flops 14155776 | bytes 14417929 | tf_op jit(solution)/shard_map/while/body/eval_jaxpr/add | solution.py:166
  187.2 1.6 copy.50
  189.5 5.8 %collective-permute-start.2 = (f32[8,1,16,256]{3,2,1,0:T(8,128)}, f32[8,1,16,256]{3,2,1,0:T(8,128)}, u32[]{:S(2)}, u32[]{:S(2)}) collective-permute-start(f32[8,1,16,256]{3,2,1,0:T(8,128)} %get-tuple-element.995), channel_id=1, source_target_pairs={{0,1},{1,2},{2,3},{3,4},{4,5},{5,6},{6,7},{8,9},{9,10},{10,11},{11... | collective-permute-start | bytes 393224 | tf_op jit(solution)/shard_map/while/body/eval_jaxpr/ppermute | solution.py:27
  198.9 7.5 %multiply_add_fusion.7 = (f32[8,16,16,256]{3,2,1,0:T(8,128)}, f32[8,16,16,256]{3,2,1,0:T(8,128)}, f32[8,16,16,256]{3,2,1,0:T(8,128)}) fusion(f32[8,16,16,256]{3,2,1,0:T(8,128)S(1)} %copy.50, f32[]{:T(128)} %bitcast.106, f32[]{:T(128)} %bitcast.107, f32[8,16,16,256]{3,2,1,0:T(8,128)} %get-tuple-element.1066, ...), kind=kLoop, calls=%fused_computation.70.clone.1 | loop fusion | flops 14155776 | bytes 14417929 | tf_op jit(solution)/shard_map/while/body/eval_jaxpr/add | solution.py:166
  206.4 5.0 %broadcast_multiply_fusion.4 = (f32[8,16,16,256]{3,2,1,0:T(8,128)}, f32[8,16,16,256]{3,2,1,0:T(8,128)}) fusion(f32[16,16,256]{2,1,0:T(8,128)} %add.657, f32[8,16,16,256]{3,2,1,0:T(8,128)} %get-tuple-element.571, f32[8,16,16,256]{3,2,1,0:T(8,128)} %get-tuple-element.572), kind=kLoop, calls=%fused_computation.183 | loop fusion | flops 1572864 | bytes 8650752 | tf_op jit(solution)/shard_map/mul | solution.py:158
  211.4 76.0 %while.65 = (s32[]{:T(128)}, f32[8,16,16,256]{3,2,1,0:T(8,128)}, f32[8,16,16,256]{3,2,1,0:T(8,128)}, f32[8,16,16,256]{3,2,1,0:T(8,128)}, f32[16,16,256]{2,1,0:T(...) while((s32[]{:T(128)}, f32[8,16,16,256]{3,2,1,0:T(8,128)}, ...), condition=%wide.region_7.8_spmd.clone.clone, body=%wide.region_6.7_spmd.sunk.clone.clone.sunk | while | flops 14811139 | bytes 23068904 | solution.py:169
  211.4 1.6 copy.51
  213.7 5.8 %collective-permute-start.4 = (f32[8,1,16,256]{3,2,1,0:T(8,128)}, f32[8,1,16,256]{3,2,1,0:T(8,128)}, u32[]{:S(2)}, u32[]{:S(2)}) collective-permute-start(f32[8,1,16,256]{3,2,1,0:T(8,128)} %get-tuple-element.1013), channel_id=1, source_target_pairs={{0,1},{1,2},{2,3},{3,4},{4,5},{5,6},{6,7},{8,9},{9,10},{10,11},{11... | collective-permute-start | bytes 393224 | tf_op jit(solution)/shard_map/while/body/eval_jaxpr/ppermute | solution.py:27
  223.1 7.0 %multiply_add_fusion.8 = (f32[8,16,16,256]{3,2,1,0:T(8,128)}, f32[8,16,16,256]{3,2,1,0:T(8,128)}, f32[8,16,16,256]{3,2,1,0:T(8,128)}) fusion(f32[8,16,16,256]{3,2,1,0:T(8,128)S(1)} %copy.51, f32[]{:T(128)} %bitcast.108, f32[]{:T(128)} %bitcast.109, f32[8,16,16,256]{3,2,1,0:T(8,128)} %get-tuple-element.1099, ...), kind=kLoop, calls=%fused_computation.111.clone.1 | loop fusion | flops 14155776 | bytes 14417929 | tf_op jit(solution)/shard_map/while/body/eval_jaxpr/add | solution.py:166
  230.1 1.6 copy.51
  232.4 5.8 %collective-permute-start.4 = (f32[8,1,16,256]{3,2,1,0:T(8,128)}, f32[8,1,16,256]{3,2,1,0:T(8,128)}, u32[]{:S(2)}, u32[]{:S(2)}) collective-permute-start(f32[8,1,16,256]{3,2,1,0:T(8,128)} %get-tuple-element.1013), channel_id=1, source_target_pairs={{0,1},{1,2},{2,3},{3,4},{4,5},{5,6},{6,7},{8,9},{9,10},{10,11},{11... | collective-permute-start | bytes 393224 | tf_op jit(solution)/shard_map/while/body/eval_jaxpr/ppermute | solution.py:27
  241.8 7.4 %multiply_add_fusion.8 = (f32[8,16,16,256]{3,2,1,0:T(8,128)}, f32[8,16,16,256]{3,2,1,0:T(8,128)}, f32[8,16,16,256]{3,2,1,0:T(8,128)}) fusion(f32[8,16,16,256]{3,2,1,0:T(8,128)S(1)} %copy.51, f32[]{:T(128)} %bitcast.108, f32[]{:T(128)} %bitcast.109, f32[8,16,16,256]{3,2,1,0:T(8,128)} %get-tuple-element.1099, ...), kind=kLoop, calls=%fused_computation.111.clone.1 | loop fusion | flops 14155776 | bytes 14417929 | tf_op jit(solution)/shard_map/while/body/eval_jaxpr/add | solution.py:166
  249.2 1.6 copy.51
  251.5 5.8 %collective-permute-start.4 = (f32[8,1,16,256]{3,2,1,0:T(8,128)}, f32[8,1,16,256]{3,2,1,0:T(8,128)}, u32[]{:S(2)}, u32[]{:S(2)}) collective-permute-start(f32[8,1,16,256]{3,2,1,0:T(8,128)} %get-tuple-element.1013), channel_id=1, source_target_pairs={{0,1},{1,2},{2,3},{3,4},{4,5},{5,6},{6,7},{8,9},{9,10},{10,11},{11... | collective-permute-start | bytes 393224 | tf_op jit(solution)/shard_map/while/body/eval_jaxpr/ppermute | solution.py:27
  260.9 7.4 %multiply_add_fusion.8 = (f32[8,16,16,256]{3,2,1,0:T(8,128)}, f32[8,16,16,256]{3,2,1,0:T(8,128)}, f32[8,16,16,256]{3,2,1,0:T(8,128)}) fusion(f32[8,16,16,256]{3,2,1,0:T(8,128)S(1)} %copy.51, f32[]{:T(128)} %bitcast.108, f32[]{:T(128)} %bitcast.109, f32[8,16,16,256]{3,2,1,0:T(8,128)} %get-tuple-element.1099, ...), kind=kLoop, calls=%fused_computation.111.clone.1 | loop fusion | flops 14155776 | bytes 14417929 | tf_op jit(solution)/shard_map/while/body/eval_jaxpr/add | solution.py:166
  268.3 1.6 copy.51
  270.6 5.8 %collective-permute-start.4 = (f32[8,1,16,256]{3,2,1,0:T(8,128)}, f32[8,1,16,256]{3,2,1,0:T(8,128)}, u32[]{:S(2)}, u32[]{:S(2)}) collective-permute-start(f32[8,1,16,256]{3,2,1,0:T(8,128)} %get-tuple-element.1013), channel_id=1, source_target_pairs={{0,1},{1,2},{2,3},{3,4},{4,5},{5,6},{6,7},{8,9},{9,10},{10,11},{11... | collective-permute-start | bytes 393224 | tf_op jit(solution)/shard_map/while/body/eval_jaxpr/ppermute | solution.py:27
  280.0 7.4 %multiply_add_fusion.8 = (f32[8,16,16,256]{3,2,1,0:T(8,128)}, f32[8,16,16,256]{3,2,1,0:T(8,128)}, f32[8,16,16,256]{3,2,1,0:T(8,128)}) fusion(f32[8,16,16,256]{3,2,1,0:T(8,128)S(1)} %copy.51, f32[]{:T(128)} %bitcast.108, f32[]{:T(128)} %bitcast.109, f32[8,16,16,256]{3,2,1,0:T(8,128)} %get-tuple-element.1099, ...), kind=kLoop, calls=%fused_computation.111.clone.1 | loop fusion | flops 14155776 | bytes 14417929 | tf_op jit(solution)/shard_map/while/body/eval_jaxpr/add | solution.py:166
  287.4 2.7 add.658
  290.1 5.2 %collective-permute-start.13 = (f32[8,1,16,256]{3,2,1,0:T(8,128)S(1)}, f32[8,1,16,256]{3,2,1,0:T(8,128)S(1)}, u32[]{:S(2)}, u32[]{:S(2)}) collective-permute-start(f32[8,1,16,256]{3,2,1,0:T(8,128)S(1)} %get-tuple-element.818), channel_id=1, source_target_pairs={{0,1},{1,2},{2,3},{3,4},{4,5},{5,6},{6,7},{8,9},{9,10},{10,11},{11... | collective-permute-start | bytes 393224 | tf_op jit(solution)/shard_map/ppermute | solution.py:27
  296.6 1.9 collective-permute-done.14
  300.3 3.2 fusion.107
  303.6 89.3 %all-reduce.20.cloned.1.call-done = f32[8,16,16,256]{3,2,1,0:T(8,128)} async-done(((f32[8,16,16,256]{3,2,1,0:T(8,128)}), f32[8,16,16,256]{3,2,1,0:T(8,128)}) %all-reduce.20.cloned.1.call-update) | async-done | bytes 2097168 | tf_op jit(solution)/shard_map/psum | solution.py:186
  392.9 1.9 constant_dynamic-slice_fusion
  (167 shorter events, 55.6 us)
Async XLA Ops:
  6.5 386.4 %all-reduce.20.cloned.1.call-start = ((), (), s32[]{:S(2)}) async-start(), calls=%async_computation | async-start | bytes 4194304 | tf_op jit(solution)/shard_map/psum | solution.py:186
  6.5 18.1 %collective-permute-start.6 = (f32[2,16,16,256]{3,2,1,0:T(8,128)}, f32[2,16,16,256]{3,2,1,0:T(8,128)S(1)}, u32[]{:S(2)}, u32[]{:S(2)}) collective-permute-start(f32[2,16,16,256]{3,2,1,0:T(8,128)} %param.15), channel_id=1, source_target_pairs={{0,8},{8,16},{16,24},{24,0},{1,9},{9,17},{17,25},{25,1},{2,10},{10... | collective-permute-start | bytes 1572872 | tf_op jit(solution)/shard_map/ppermute | solution.py:122
  9.6 25.1 %collective-permute-start.8 = (f32[2,16,16,256]{3,2,1,0:T(8,128)}, f32[2,16,16,256]{3,2,1,0:T(8,128)S(1)}, u32[]{:S(2)}, u32[]{:S(2)}) collective-permute-start(f32[2,16,16,256]{3,2,1,0:T(8,128)} %param.15), channel_id=1, source_target_pairs={{8,0},{16,8},{24,16},{0,24},{9,1},{17,9},{25,17},{1,25},{10,2},{18... | collective-permute-start | bytes 1572872 | tf_op jit(solution)/shard_map/ppermute | solution.py:126
  24.6 21.6 %copy-start.13 = (f32[2,16,16,256]{3,2,1,0:T(8,128)}, f32[2,16,16,256]{3,2,1,0:T(8,128)S(1)}, u32[]{:S(2)}) copy-start(f32[2,16,16,256]{3,2,1,0:T(8,128)S(1)} %collective-permute-done.6) | copy-start | bytes 1572868
  24.6 21.6 %collective-permute-start.7 = (f32[2,16,16,256]{3,2,1,0:T(8,128)S(1)}, f32[2,16,16,256]{3,2,1,0:T(8,128)S(1)}, u32[]{:S(2)}, u32[]{:S(2)}) collective-permute-start(f32[2,16,16,256]{3,2,1,0:T(8,128)S(1)} %collective-permute-done.6), channel_id=1, source_target_pairs={{0,8},{8,16},{16,24},{24,0},{1,9},{9,17},{17,25},{25,1},{2,10},{10... | collective-permute-start | bytes 1572872 | tf_op jit(solution)/shard_map/ppermute | solution.py:122
  26.6 35.6 %copy-start = (f32[1,16,16,256]{3,2,1,0:T(8,128)}, f32[1,16,16,256]{3,2,1,0:T(8,128)S(1)}, u32[]{:S(2)}) copy-start(f32[1,16,16,256]{3,2,1,0:T(8,128)S(1)} %get-tuple-element.823) | copy-start | bytes 786436
  34.7 11.6 %copy-start.14 = (f32[2,16,16,256]{3,2,1,0:T(8,128)}, f32[2,16,16,256]{3,2,1,0:T(8,128)S(1)}, u32[]{:S(2)}) copy-start(f32[2,16,16,256]{3,2,1,0:T(8,128)S(1)} %collective-permute-done.8) | copy-start | bytes 1572868
  46.3 0.8 copy-start.15
  52.9 3.5 copy-start.16
  52.9 3.5 copy-start.17
  53.7 6.2 %collective-permute-start.10 = (f32[9,2,16,256]{3,2,1,0:T(8,128)}, f32[9,2,16,256]{3,2,1,0:T(8,128)S(1)}, u32[]{:S(2)}, u32[]{:S(2)}) collective-permute-start(f32[9,2,16,256]{3,2,1,0:T(8,128)} %get-tuple-element.816), channel_id=1, source_target_pairs={{0,1},{1,2},{2,3},{3,4},{4,5},{5,6},{6,7},{8,9},{9,10},{10,11},{11... | collective-permute-start | bytes 884744 | tf_op jit(solution)/shard_map/ppermute | solution.py:27
  55.0 5.4 %collective-permute-start.9 = (f32[9,2,16,256]{3,2,1,0:T(8,128)}, f32[9,2,16,256]{3,2,1,0:T(8,128)S(1)}, u32[]{:S(2)}, u32[]{:S(2)}) collective-permute-start(f32[9,2,16,256]{3,2,1,0:T(8,128)} %get-tuple-element.817), channel_id=1, source_target_pairs={{1,0},{2,1},{3,2},{4,3},{5,4},{6,5},{7,6},{9,8},{10,9},{11,10},{12... | collective-permute-start | bytes 884744 | tf_op jit(solution)/shard_map/ppermute | solution.py:29
  59.9 3.1 copy-start.2
  60.4 0.7 copy-start.4
  62.2 0.8 copy-start.18
  62.2 0.8 copy-start.19
  64.0 9.9 %collective-permute-start = (f32[1,1,16,256]{3,2,1,0:T(8,128)S(1)}, f32[1,1,16,256]{3,2,1,0:T(8,128)S(1)}, u32[]{:S(2)}, u32[]{:S(2)}) collective-permute-start(f32[1,1,16,256]{3,2,1,0:T(8,128)S(1)} %get-tuple-element.979), channel_id=1, source_target_pairs={{0,1},{1,2},{2,3},{3,4},{4,5},{5,6},{6,7},{8,9},{9,10},{10,11},{11... | collective-permute-start | bytes 49160 | tf_op jit(solution)/shard_map/while/body/eval_jaxpr/ppermute | solution.py:27
  71.4 3.1 collective-permute-start.1
  78.9 6.8 %collective-permute-start = (f32[1,1,16,256]{3,2,1,0:T(8,128)S(1)}, f32[1,1,16,256]{3,2,1,0:T(8,128)S(1)}, u32[]{:S(2)}, u32[]{:S(2)}) collective-permute-start(f32[1,1,16,256]{3,2,1,0:T(8,128)S(1)} %get-tuple-element.979), channel_id=1, source_target_pairs={{0,1},{1,2},{2,3},{3,4},{4,5},{5,6},{6,7},{8,9},{9,10},{10,11},{11... | collective-permute-start | bytes 49160 | tf_op jit(solution)/shard_map/while/body/eval_jaxpr/ppermute | solution.py:27
  83.1 3.1 collective-permute-start.1
  90.7 7.3 %collective-permute-start = (f32[1,1,16,256]{3,2,1,0:T(8,128)S(1)}, f32[1,1,16,256]{3,2,1,0:T(8,128)S(1)}, u32[]{:S(2)}, u32[]{:S(2)}) collective-permute-start(f32[1,1,16,256]{3,2,1,0:T(8,128)S(1)} %get-tuple-element.979), channel_id=1, source_target_pairs={{0,1},{1,2},{2,3},{3,4},{4,5},{5,6},{6,7},{8,9},{9,10},{10,11},{11... | collective-permute-start | bytes 49160 | tf_op jit(solution)/shard_map/while/body/eval_jaxpr/ppermute | solution.py:27
  95.5 3.1 collective-permute-start.1
  103.1 7.4 %collective-permute-start = (f32[1,1,16,256]{3,2,1,0:T(8,128)S(1)}, f32[1,1,16,256]{3,2,1,0:T(8,128)S(1)}, u32[]{:S(2)}, u32[]{:S(2)}) collective-permute-start(f32[1,1,16,256]{3,2,1,0:T(8,128)S(1)} %get-tuple-element.979), channel_id=1, source_target_pairs={{0,1},{1,2},{2,3},{3,4},{4,5},{5,6},{6,7},{8,9},{9,10},{10,11},{11... | collective-permute-start | bytes 49160 | tf_op jit(solution)/shard_map/while/body/eval_jaxpr/ppermute | solution.py:27
  107.9 3.1 collective-permute-start.1
  115.6 8.9 %collective-permute-start.11 = (f32[1,1,16,256]{3,2,1,0:T(8,128)S(1)}, f32[1,1,16,256]{3,2,1,0:T(8,128)S(1)}, u32[]{:S(2)}, u32[]{:S(2)}) collective-permute-start(f32[1,1,16,256]{3,2,1,0:T(8,128)S(1)} %get-tuple-element.831), channel_id=1, source_target_pairs={{0,1},{1,2},{2,3},{3,4},{4,5},{5,6},{6,7},{8,9},{9,10},{10,11},{11... | collective-permute-start | bytes 49160 | tf_op jit(solution)/shard_map/ppermute | solution.py:27
  120.4 4.1 %collective-permute-start.12 = (f32[1,1,16,256]{3,2,1,0:T(8,128)S(1)}, f32[1,1,16,256]{3,2,1,0:T(8,128)S(1)}, u32[]{:S(2)}, u32[]{:S(2)}) collective-permute-start(f32[1,1,16,256]{3,2,1,0:T(8,128)S(1)} %get-tuple-element.832), channel_id=1, source_target_pairs={{1,0},{2,1},{3,2},{4,3},{5,4},{6,5},{7,6},{9,8},{10,9},{11,10},{12... | collective-permute-start | bytes 49160 | tf_op jit(solution)/shard_map/ppermute | solution.py:29
  124.5 1.4 copy-start.1
  124.5 1.4 copy-start.3
  124.5 1.4 copy-start.5
  132.2 8.1 %collective-permute-start.2 = (f32[8,1,16,256]{3,2,1,0:T(8,128)}, f32[8,1,16,256]{3,2,1,0:T(8,128)}, u32[]{:S(2)}, u32[]{:S(2)}) collective-permute-start(f32[8,1,16,256]{3,2,1,0:T(8,128)} %get-tuple-element.995), channel_id=1, source_target_pairs={{0,1},{1,2},{2,3},{3,4},{4,5},{5,6},{6,7},{8,9},{9,10},{10,11},{11... | collective-permute-start | bytes 393224 | tf_op jit(solution)/shard_map/while/body/eval_jaxpr/ppermute | solution.py:27
  136.6 3.8 collective-permute-start.3
  149.9 9.7 %collective-permute-start.2 = (f32[8,1,16,256]{3,2,1,0:T(8,128)}, f32[8,1,16,256]{3,2,1,0:T(8,128)}, u32[]{:S(2)}, u32[]{:S(2)}) collective-permute-start(f32[8,1,16,256]{3,2,1,0:T(8,128)} %get-tuple-element.995), channel_id=1, source_target_pairs={{0,1},{1,2},{2,3},{3,4},{4,5},{5,6},{6,7},{8,9},{9,10},{10,11},{11... | collective-permute-start | bytes 393224 | tf_op jit(solution)/shard_map/while/body/eval_jaxpr/ppermute | solution.py:27
  156.0 3.6 collective-permute-start.3
  169.4 10.3 %collective-permute-start.2 = (f32[8,1,16,256]{3,2,1,0:T(8,128)}, f32[8,1,16,256]{3,2,1,0:T(8,128)}, u32[]{:S(2)}, u32[]{:S(2)}) collective-permute-start(f32[8,1,16,256]{3,2,1,0:T(8,128)} %get-tuple-element.995), channel_id=1, source_target_pairs={{0,1},{1,2},{2,3},{3,4},{4,5},{5,6},{6,7},{8,9},{9,10},{10,11},{11... | collective-permute-start | bytes 393224 | tf_op jit(solution)/shard_map/while/body/eval_jaxpr/ppermute | solution.py:27
  176.1 3.6 collective-permute-start.3
  189.5 9.4 %collective-permute-start.2 = (f32[8,1,16,256]{3,2,1,0:T(8,128)}, f32[8,1,16,256]{3,2,1,0:T(8,128)}, u32[]{:S(2)}, u32[]{:S(2)}) collective-permute-start(f32[8,1,16,256]{3,2,1,0:T(8,128)} %get-tuple-element.995), channel_id=1, source_target_pairs={{0,1},{1,2},{2,3},{3,4},{4,5},{5,6},{6,7},{8,9},{9,10},{10,11},{11... | collective-permute-start | bytes 393224 | tf_op jit(solution)/shard_map/while/body/eval_jaxpr/ppermute | solution.py:27
  195.3 3.6 collective-permute-start.3
  213.7 9.4 %collective-permute-start.4 = (f32[8,1,16,256]{3,2,1,0:T(8,128)}, f32[8,1,16,256]{3,2,1,0:T(8,128)}, u32[]{:S(2)}, u32[]{:S(2)}) collective-permute-start(f32[8,1,16,256]{3,2,1,0:T(8,128)} %get-tuple-element.1013), channel_id=1, source_target_pairs={{0,1},{1,2},{2,3},{3,4},{4,5},{5,6},{6,7},{8,9},{9,10},{10,11},{11... | collective-permute-start | bytes 393224 | tf_op jit(solution)/shard_map/while/body/eval_jaxpr/ppermute | solution.py:27
  219.5 3.6 collective-permute-start.5
  232.4 9.4 %collective-permute-start.4 = (f32[8,1,16,256]{3,2,1,0:T(8,128)}, f32[8,1,16,256]{3,2,1,0:T(8,128)}, u32[]{:S(2)}, u32[]{:S(2)}) collective-permute-start(f32[8,1,16,256]{3,2,1,0:T(8,128)} %get-tuple-element.1013), channel_id=1, source_target_pairs={{0,1},{1,2},{2,3},{3,4},{4,5},{5,6},{6,7},{8,9},{9,10},{10,11},{11... | collective-permute-start | bytes 393224 | tf_op jit(solution)/shard_map/while/body/eval_jaxpr/ppermute | solution.py:27
  238.2 3.6 collective-permute-start.5
  251.5 9.4 %collective-permute-start.4 = (f32[8,1,16,256]{3,2,1,0:T(8,128)}, f32[8,1,16,256]{3,2,1,0:T(8,128)}, u32[]{:S(2)}, u32[]{:S(2)}) collective-permute-start(f32[8,1,16,256]{3,2,1,0:T(8,128)} %get-tuple-element.1013), channel_id=1, source_target_pairs={{0,1},{1,2},{2,3},{3,4},{4,5},{5,6},{6,7},{8,9},{9,10},{10,11},{11... | collective-permute-start | bytes 393224 | tf_op jit(solution)/shard_map/while/body/eval_jaxpr/ppermute | solution.py:27
  257.3 3.6 collective-permute-start.5
  270.6 9.4 %collective-permute-start.4 = (f32[8,1,16,256]{3,2,1,0:T(8,128)}, f32[8,1,16,256]{3,2,1,0:T(8,128)}, u32[]{:S(2)}, u32[]{:S(2)}) collective-permute-start(f32[8,1,16,256]{3,2,1,0:T(8,128)} %get-tuple-element.1013), channel_id=1, source_target_pairs={{0,1},{1,2},{2,3},{3,4},{4,5},{5,6},{6,7},{8,9},{9,10},{10,11},{11... | collective-permute-start | bytes 393224 | tf_op jit(solution)/shard_map/while/body/eval_jaxpr/ppermute | solution.py:27
  276.4 3.6 collective-permute-start.5
  290.1 6.5 %collective-permute-start.13 = (f32[8,1,16,256]{3,2,1,0:T(8,128)S(1)}, f32[8,1,16,256]{3,2,1,0:T(8,128)S(1)}, u32[]{:S(2)}, u32[]{:S(2)}) collective-permute-start(f32[8,1,16,256]{3,2,1,0:T(8,128)S(1)} %get-tuple-element.818), channel_id=1, source_target_pairs={{0,1},{1,2},{2,3},{3,4},{4,5},{5,6},{6,7},{8,9},{9,10},{10,11},{11... | collective-permute-start | bytes 393224 | tf_op jit(solution)/shard_map/ppermute | solution.py:27
  295.3 3.2 collective-permute-start.14
  298.9 1.0 copy-start.6
  298.9 1.0 copy-start.7
  298.9 1.1 copy-start.8
  298.9 1.2 copy-start.9
  298.9 1.2 copy-start.10
  298.9 1.3 copy-start.11
  299.0 1.4 copy-start.12
Sparse Core Ops, SparseCore 0:
  303.7 89.1 all-reduce.19
